TPU v7x, 128 devices: a whole 4x4x4 slice. The times are simulated.
128 devices in a mesh: req: 8 (over y, core), hid: 16 (over x, z).
Axes of the slice: x: 4, y: 4, z: 4, core: 2. Of those that a mesh axis runs over, the one named last changes fastest.
Arguments:
- tokens: bfloat16 [24576, 1536], P(('req', 'hid')), may hold values from -6 to 6
- segment: int32 [24576], P(('req', 'hid')), may hold values from 0 to 35, as said below
- attn_gain: float32 [1536], replicated, may hold values from 0.1 to 1.9
- w_query: bfloat16 [1536, 1536], replicated, may hold values from -0.2 to 0.2
- w_key: bfloat16 [1536, 512], replicated, may hold values from -0.2 to 0.2
- w_value: bfloat16 [1536, 512], replicated, may hold values from -0.15625 to 0.15625
- q_gain: float32 [64], replicated, may hold values from 0.5 to 6
- k_gain: float32 [64], replicated, may hold values from 0.5 to 6
- w_out: bfloat16 [1536, 1536], replicated, may hold values from -0.15625 to 0.15625
- ffn_gain: float32 [1536], replicated, may hold values from 0.1 to 1.9
- w_gate: bfloat16 [4608, 1536], P(('req', 'hid')), may hold values from -0.15625 to 0.15625
- w_up: bfloat16 [4608, 1536], P(('req', 'hid')), may hold values from -0.15625 to 0.15625
- w_down: bfloat16 [4608, 1536], P(('req', 'hid')), may hold values from -0.09375 to 0.09375
Outputs:
- mixed: bfloat16 [24576, 1536], P(('req', 'hid'))
- kv_cache: bfloat16 [24576, 1024], P(('req', 'hid'))
Inputs may be any that keep to these rules, and one draw needn't show every extreme that they name: Segment ids never fall along the tokens and start at 0. A segment never crosses a boundary between aligned blocks of 3072 tokens; the first block is one segment of exactly 3072 tokens, and every later block holds exactly five segments.
All inputs are finite; a program needn't handle non-finite values.
Results may differ from a plain program's by a relative error of at most 0.015.
Values may be sent and summed in bfloat16 or wider, within the bound.
No kernel may reach another device: no remote copies, remote signals or barrier semaphores. Data moves between devices by JAX's collectives and lax.ppermute only.
A program may use at most 128 MiB of HBM per device.

v0:
```python
import jax
import jax.numpy as jnp
from jax import lax
from jax.sharding import PartitionSpec as P

H = 24
KVH = 8
HD = 64
EPSILON = 1e-05
ROPE_BASE = 1000000.0
NEG_FILL = -1e30
SCORE_SCALE = 0.125


def rms_scale(values, gain):
    mean_sq = jnp.mean(values * values, axis=-1, keepdims=True)
    return values * lax.rsqrt(mean_sq + EPSILON) * gain


def seg_positions(seg_ids):
    indices = jnp.arange(seg_ids.shape[0], dtype=jnp.int32)
    is_first = jnp.concatenate([jnp.ones((1,), bool), seg_ids[1:] != seg_ids[:-1]])
    seg_begin = lax.cummax(jnp.where(is_first, indices, jnp.zeros_like(indices)), axis=0)
    return indices - seg_begin


def rotate(heads, positions):
    half_dim = heads.shape[-1] // 2
    inv_freq = ROPE_BASE ** (-(jnp.arange(half_dim, dtype=jnp.float32) * 2.0) / (2.0 * half_dim))
    angles = positions.astype(jnp.float32)[:, None] * inv_freq[None, :]
    cos_val = jnp.cos(angles)[:, None, :]
    sin_val = jnp.sin(angles)[:, None, :]
    left = heads[..., :half_dim]
    right = heads[..., half_dim:]
    return jnp.concatenate(
        [left * cos_val - right * sin_val, right * cos_val + left * sin_val], axis=-1
    )


def block_length(shard_rows):
    return 4 * shard_rows


def key_block(running, key_blk, val_blk, key_idx, q_grid, seg_start, query_idx):
    run_peak, run_total, run_acc = running
    k_grid = key_blk.reshape(-1, KVH, HD).transpose(1, 0, 2)
    v_grid = val_blk.reshape(-1, KVH, HD).transpose(1, 0, 2)
    scores = (
        jnp.einsum("kgqd,kcd->kgqc", q_grid, k_grid, preferred_element_type=jnp.float32)
        * SCORE_SCALE
    )
    allowed = (key_idx[None, :] <= query_idx[:, None]) & (key_idx[None, :] >= seg_start[:, None])
    scores = jnp.where(allowed, scores, NEG_FILL)
    new_peak = jnp.maximum(run_peak, jnp.max(scores, axis=-1))
    weights = jnp.where(allowed, jnp.exp(scores - new_peak[..., None]), 0.0)
    factor = jnp.exp(run_peak - new_peak)
    new_total = run_total * factor + jnp.sum(weights, axis=-1)
    product = jnp.einsum(
        "kgqc,kcd->kgqd", weights.astype(jnp.bfloat16), v_grid, preferred_element_type=jnp.float32
    )
    return (new_peak, new_total, run_acc * factor[..., None] + product)


def unit_terms(pieces, gathered):
    gate_part, up_part, down_part = pieces
    contract = (((1,), (1,)), ((), ()))
    gate_act = lax.dot_general(gathered, gate_part, contract, preferred_element_type=jnp.float32)
    up_act = lax.dot_general(gathered, up_part, contract, preferred_element_type=jnp.float32)
    hidden = (jax.nn.silu(gate_act) * up_act).astype(jnp.bfloat16)
    return jnp.dot(hidden, down_part, preferred_element_type=jnp.float32)


def join_runs(left, right):
    l_last, l_trail, l_full = left
    r_last, r_trail, r_full = right
    same = (l_last == r_last) & (r_full > 0)
    trail = r_trail + jnp.where(same, l_trail, 0)
    full = jnp.where(same & (l_full > 0), 1, 0)
    return (r_last, trail, full)


def group_positions(seg_ids, axis):
    count = lax.psum(1, axis)
    me = lax.axis_index(axis)
    rows = seg_ids.shape[0]
    last = seg_ids[rows - 1]
    trail = jnp.sum((seg_ids == last).astype(jnp.int32))
    full = (seg_ids[0] == last).astype(jnp.int32)
    summary = jnp.stack([last, trail, full])
    shift = 1
    while shift < count:
        pairs = [(src, src + shift) for src in range(count - shift)]
        got = lax.ppermute(summary, axis, pairs)
        joined = jnp.stack(
            join_runs((got[0], got[1], got[2]), (summary[0], summary[1], summary[2]))
        )
        summary = jnp.where(me >= shift, joined, summary)
        shift *= 2
    before = lax.ppermute(summary, axis, [(src, src + 1) for src in range(count - 1)])
    local = seg_positions(seg_ids)
    lead = local == jnp.arange(rows, dtype=jnp.int32)
    carry = jnp.where((me > 0) & (before[0] == seg_ids[0]), before[1], 0)
    return local + jnp.where(lead, carry, 0)


def per_device(
    tokens,
    segment,
    attn_gain,
    w_query,
    w_key,
    w_value,
    q_gain,
    k_gain,
    w_out,
    ffn_gain,
    w_gate,
    w_up,
    w_down,
):
    shard_rows = tokens.shape[0]
    groups = H // KVH
    row_base = lax.axis_index("hid") * shard_rows
    positions = group_positions(segment, "hid")
    query_idx = row_base + jnp.arange(shard_rows, dtype=jnp.int32)
    seg_start = query_idx - positions
    resid = tokens.astype(jnp.float32)
    normed = rms_scale(resid, attn_gain).astype(jnp.bfloat16)
    q_raw = jnp.dot(normed, w_query, preferred_element_type=jnp.float32).reshape(shard_rows, H, HD)
    k_raw = jnp.dot(normed, w_key, preferred_element_type=jnp.float32).reshape(shard_rows, KVH, HD)
    queries = rotate(rms_scale(q_raw, q_gain), positions).astype(jnp.bfloat16)
    key_heads = (
        rotate(rms_scale(k_raw, k_gain), positions)
        .astype(jnp.bfloat16)
        .reshape(shard_rows, KVH * HD)
    )
    values = jnp.dot(normed, w_value, preferred_element_type=jnp.float32).astype(jnp.bfloat16)
    kv_cache = jnp.concatenate([key_heads, values], axis=1)
    q_grid = queries.reshape(shard_rows, KVH, groups, HD).transpose(1, 2, 0, 3)
    start_state = (
        jnp.full((KVH, groups, shard_rows), NEG_FILL, jnp.float32),
        jnp.zeros((KVH, groups, shard_rows), jnp.float32),
        jnp.zeros((KVH, groups, shard_rows, HD), jnp.float32),
    )
    hid_count = lax.psum(1, "hid")
    pieces = [kv_cache, w_gate, w_up, w_down]
    sizes = [p.size for p in pieces]
    bundle = lax.all_gather(
        jnp.concatenate([p.reshape(-1) for p in pieces]), "hid", axis=0, tiled=False
    )
    cuts = [sum(sizes[:i]) for i in range(len(sizes) + 1)]
    parts = [
        bundle[:, cuts[i] : cuts[i + 1]].reshape((hid_count * p.shape[0],) + p.shape[1:])
        for i, p in enumerate(pieces)
    ]
    kv_part, gate_rows, up_rows, down_rows = parts
    key_part = kv_part[:, : KVH * HD]
    val_part = kv_part[:, KVH * HD :]
    key_count = key_part.shape[0]
    blk_len = block_length(shard_rows)

    def one_block(block_idx, state_in):
        offset = jnp.asarray(block_idx, jnp.int32) * blk_len
        local_off = jnp.asarray(block_idx, jnp.int32) * blk_len
        key_blk = lax.dynamic_slice_in_dim(key_part, local_off, blk_len)
        val_blk = lax.dynamic_slice_in_dim(val_part, local_off, blk_len)
        key_idx = offset + jnp.arange(blk_len, dtype=jnp.int32)
        return key_block(state_in, key_blk, val_blk, key_idx, q_grid, seg_start, query_idx)

    run_peak, run_total, run_acc = lax.fori_loop(0, key_count // blk_len, one_block, start_state)
    attended = (
        (run_acc / run_total[..., None])
        .transpose(2, 0, 1, 3)
        .reshape(shard_rows, H * HD)
        .astype(jnp.bfloat16)
    )
    after_attn = (resid + jnp.dot(attended, w_out, preferred_element_type=jnp.float32)).astype(
        jnp.bfloat16
    )
    after_f32 = lax.optimization_barrier(after_attn).astype(jnp.float32)
    mlp_in = rms_scale(after_f32, ffn_gain).astype(jnp.bfloat16)
    gathered = lax.all_gather(mlp_in, "req", axis=0, tiled=True)
    unit_sum = unit_terms((gate_rows, up_rows, down_rows), gathered)
    own_share = lax.psum_scatter(
        unit_sum.astype(jnp.bfloat16), "req", scatter_dimension=0, tiled=True
    ).astype(jnp.float32)
    mixed = (after_f32 + own_share).astype(jnp.bfloat16)
    return (mixed, kv_cache)


def solution(mesh):
    placed = (
        P(("req", "hid"), None),
        P(("req", "hid")),
        P(),
        P(),
        P(),
        P(),
        P(),
        P(),
        P(),
        P(),
        P(("req", "hid"), None),
        P(("req", "hid"), None),
        P(("req", "hid"), None),
    )
    return jax.shard_map(
        per_device,
        mesh=mesh,
        in_specs=placed,
        out_specs=(P(("req", "hid"), None), P(("req", "hid"), None)),
        check_vma=False,
    )
```

profile of v0, /device:TPU:0, one launch (start us, length us, event | category | flops | bytes accessed | tf_op | source)
XLA Modules:
  0.0 388.1 jit_solution(17005629761590699012)
XLA Ops:
  7.2 1.4 fusion.34
  8.6 2.0 fusion.24
  11.9 1.3 pad_add_fusion
  13.3 3.9 %collective-permute-start = (s32[3]{0:T(128)S(1)}, s32[3]{0:T(128)S(1)}, u32[]{:S(2)}, u32[]{:S(2)}) collective-permute-start(s32[3]{0:T(128)S(1)} %pad_add_fusion), channel_id=1, source_target_pairs={{0,1},{1,2},{2,3},{3,4},{4,5},{5,6},{6,7},{7,8},{8,9},{9,10},{10,1... | collective-permute-start | bytes 44 | tf_op jit(solution)/shard_map/ppermute | solution.py:93
  23.3 2.1 convolution_convert_fusion.1
  30.2 1.3 broadcast_select_fusion
  32.3 5.5 %collective-permute-start.1 = (s32[3]{0:T(128)S(1)}, s32[3]{0:T(128)S(1)}, u32[]{:S(2)}, u32[]{:S(2)}) collective-permute-start(s32[3]{0:T(128)S(1)} %broadcast_select_fusion), channel_id=1, source_target_pairs={{0,2},{1,3},{2,4},{3,5},{4,6},{5,7},{6,8},{7,9},{8,10},{9,11},{10,... | collective-permute-start | bytes 44 | tf_op jit(solution)/shard_map/ppermute | solution.py:93
  43.0 2.0 broadcast_select_fusion.1
  45.6 4.4 %collective-permute-start.2 = (s32[3]{0:T(128)S(1)}, s32[3]{0:T(128)S(1)}, u32[]{:S(2)}, u32[]{:S(2)}) collective-permute-start(s32[3]{0:T(128)S(1)} %broadcast_select_fusion.1), channel_id=1, source_target_pairs={{0,4},{1,5},{2,6},{3,7},{4,8},{5,9},{6,10},{7,11},{8,12},{9,13},{1... | collective-permute-start | bytes 44 | tf_op jit(solution)/shard_map/ppermute | solution.py:93
  55.3 2.7 broadcast_select_fusion.2
  58.6 5.7 %collective-permute-start.3 = (s32[3]{0:T(128)S(1)}, s32[3]{0:T(128)S(1)}, u32[]{:S(2)}, u32[]{:S(2)}) collective-permute-start(s32[3]{0:T(128)S(1)} %broadcast_select_fusion.2), channel_id=1, source_target_pairs={{0,8},{1,9},{2,10},{3,11},{4,12},{5,13},{6,14},{7,15},{16,24},{17,... | collective-permute-start | bytes 44 | tf_op jit(solution)/shard_map/ppermute | solution.py:93
  69.4 3.2 broadcast_select_fusion.3
  72.6 3.8 collective-permute-start.4
  76.5 1.3 collective-permute-done.4
  81.9 4.3 %fusion.27 = f32[192,1536]{0,1:T(8,128)S(1)} fusion(bf16[1536,1536]{1,0:T(8,128)(2,1)} %param.18, bf16[192,1536]{1,0:T(8,128)(2,1)S(1)} %copy-done.12, f32[1536]{0:T(1024)S(1)} %copy-done.17, f32[192]{0:T(256)S(1)} %add_rsqrt_fusion.3), kind=kOutput, calls=%fused_computation.76 | convolution fusion | flops 907149312 | bytes 6494976 | tf_op jit(solution)/shard_map/dot_general | solution.py:129
  87.2 82.5 %all-gather.6.cloned.1.call-done = bf16[5799936]{0:T(1024)(128)(2,1)} async-done(((bf16[362496]{0:T(1024)(128)(2,1)}), bf16[5799936]{0:T(1024)(128)(2,1)}) %all-gather.6.cloned.1.call-update) | async-done | bytes 11599888 | tf_op jit(solution)/shard_map/all_gather | solution.py:148
  169.7 15.1 %reshape.228 = bf16[16,362496]{1,0:T(8,128)(2,1)} reshape(bf16[5799936]{0:T(1024)(128)(2,1)} %all-gather.6.cloned.1.call-done) | data formatting | bytes 23199744 | tf_op jit(solution)/shard_map/all_gather | solution.py:148
  184.8 6.4 %slice.164 = bf16[16,196608]{1,0:T(8,128)(2,1)} slice(bf16[16,362496]{1,0:T(8,128)(2,1)} %reshape.228), slice={[0:16], [0:196608]} | slice | bytes 12582912 | tf_op jit(solution)/shard_map/slice | solution.py:153
  191.2 6.4 %reshape.223 = bf16[3072,1024]{1,0:T(8,128)(2,1)} reshape(bf16[16,196608]{1,0:T(8,128)(2,1)} %slice.164) | data formatting | bytes 12582912 | tf_op jit(solution)/shard_map/reshape | solution.py:153
  197.6 5.9 %fusion.33 = (bf16[3072,512]{1,0:T(8,128)(2,1)}, bf16[3072,512]{1,0:T(8,128)(2,1)}) fusion(bf16[3072,1024]{1,0:T(8,128)(2,1)} %reshape.223), kind=kLoop, calls=%fused_computation.79 | loop fusion | bytes 12582912 | tf_op jit(solution)/shard_map/slice | solution.py:158
  203.6 75.3 %while.18 = (s32[]{:T(128)}, f32[8,3,192]{2,1,0:T(4,128)S(1)}, f32[8,3,192]{2,1,0:T(4,128)}, f32[8,3,192,64]{2,3,1,0:T(8,128)}, s32[192]{0:T(256)S(1)}, /*index=...) while((s32[]{:T(128)}, f32[8,3,192]{2,1,0:T(4,128)S(1)}, ...), condition=%wide.region_9.10_spmd.clone, body=%wide.region_6.9_spmd.clone.sunk | while | flops 953327040 | bytes 120382040 | solution.py:170
  203.8 1.5 constant_dynamic-slice_fusion.3
  205.8 3.0 fusion.70
  208.8 4.7 %fusion.71 = f32[8,3,192]{2,1,0:T(4,128)S(1)} fusion(f32[8,768,3,192]{1,3,2,0:T(8,128)S(1)} %get-tuple-element.337, f32[8,3,192]{2,1,0:T(4,128)S(1)} %select_maximum_fusion.2, pred[192,768]{1,0:T(8,128)(4,1)S(1)} %compare_and_fusion.2), kind=kLoop, calls=%fused_computation.5.clone.1 | loop fusion | flops 17690112 | bytes 14340096 | tf_op jit(solution)/shard_map/while/body/eval_jaxpr/reduce_sum | solution.py:57
  214.1 7.1 %fusion.73 = f32[8,3,192,64]{2,3,1,0:T(8,128)S(1)} fusion(f32[8,3,192,64]{2,3,1,0:T(8,128)S(1)} %copy-done.6, bf16[8,768,64,1]{1,2,3,0:T(8,128)(2,1)S(1)} %bitcast.87, f32[8,768,3,192]{1,3,2,0:T(8,128)} %copy-done.2, f32[8,3,192]{2,1,0:T(4,128)S(1)} %select_maximum_fusion.2, pred[192,768]{1,0:T(8,128)(4,1)S(1)} %compare_and_fusion.2, ...), kind=kOutput, calls=%fused_computation.9.clone.1 | convolution fusion | flops 471564288 | bytes 17485824 | tf_op jit(solution)/shard_map/while/body/eval_jaxpr/kgqc,kcd->kgqd/dot_general | solution.py:58
  222.6 1.5 constant_dynamic-slice_fusion.3
  224.6 3.0 fusion.70
  227.7 4.7 %fusion.71 = f32[8,3,192]{2,1,0:T(4,128)S(1)} fusion(f32[8,768,3,192]{1,3,2,0:T(8,128)S(1)} %get-tuple-element.337, f32[8,3,192]{2,1,0:T(4,128)S(1)} %select_maximum_fusion.2, pred[192,768]{1,0:T(8,128)(4,1)S(1)} %compare_and_fusion.2), kind=kLoop, calls=%fused_computation.5.clone.1 | loop fusion | flops 17690112 | bytes 14340096 | tf_op jit(solution)/shard_map/while/body/eval_jaxpr/reduce_sum | solution.py:57
  233.0 7.1 %fusion.73 = f32[8,3,192,64]{2,3,1,0:T(8,128)S(1)} fusion(f32[8,3,192,64]{2,3,1,0:T(8,128)S(1)} %copy-done.6, bf16[8,768,64,1]{1,2,3,0:T(8,128)(2,1)S(1)} %bitcast.87, f32[8,768,3,192]{1,3,2,0:T(8,128)} %copy-done.2, f32[8,3,192]{2,1,0:T(4,128)S(1)} %select_maximum_fusion.2, pred[192,768]{1,0:T(8,128)(4,1)S(1)} %compare_and_fusion.2, ...), kind=kOutput, calls=%fused_computation.9.clone.1 | convolution fusion | flops 471564288 | bytes 17485824 | tf_op jit(solution)/shard_map/while/body/eval_jaxpr/kgqc,kcd->kgqd/dot_general | solution.py:58
  241.4 1.5 constant_dynamic-slice_fusion.3
  243.5 3.0 fusion.70
  246.5 4.7 %fusion.71 = f32[8,3,192]{2,1,0:T(4,128)S(1)} fusion(f32[8,768,3,192]{1,3,2,0:T(8,128)S(1)} %get-tuple-element.337, f32[8,3,192]{2,1,0:T(4,128)S(1)} %select_maximum_fusion.2, pred[192,768]{1,0:T(8,128)(4,1)S(1)} %compare_and_fusion.2), kind=kLoop, calls=%fused_computation.5.clone.1 | loop fusion | flops 17690112 | bytes 14340096 | tf_op jit(solution)/shard_map/while/body/eval_jaxpr/reduce_sum | solution.py:57
  251.8 7.1 %fusion.73 = f32[8,3,192,64]{2,3,1,0:T(8,128)S(1)} fusion(f32[8,3,192,64]{2,3,1,0:T(8,128)S(1)} %copy-done.6, bf16[8,768,64,1]{1,2,3,0:T(8,128)(2,1)S(1)} %bitcast.87, f32[8,768,3,192]{1,3,2,0:T(8,128)} %copy-done.2, f32[8,3,192]{2,1,0:T(4,128)S(1)} %select_maximum_fusion.2, pred[192,768]{1,0:T(8,128)(4,1)S(1)} %compare_and_fusion.2, ...), kind=kOutput, calls=%fused_computation.9.clone.1 | convolution fusion | flops 471564288 | bytes 17485824 | tf_op jit(solution)/shard_map/while/body/eval_jaxpr/kgqc,kcd->kgqd/dot_general | solution.py:58
  260.3 1.5 constant_dynamic-slice_fusion.3
  262.3 3.0 fusion.70
  265.3 4.7 %fusion.71 = f32[8,3,192]{2,1,0:T(4,128)S(1)} fusion(f32[8,768,3,192]{1,3,2,0:T(8,128)S(1)} %get-tuple-element.337, f32[8,3,192]{2,1,0:T(4,128)S(1)} %select_maximum_fusion.2, pred[192,768]{1,0:T(8,128)(4,1)S(1)} %compare_and_fusion.2), kind=kLoop, calls=%fused_computation.5.clone.1 | loop fusion | flops 17690112 | bytes 14340096 | tf_op jit(solution)/shard_map/while/body/eval_jaxpr/reduce_sum | solution.py:57
  270.6 7.1 %fusion.73 = f32[8,3,192,64]{2,3,1,0:T(8,128)S(1)} fusion(f32[8,3,192,64]{2,3,1,0:T(8,128)S(1)} %copy-done.6, bf16[8,768,64,1]{1,2,3,0:T(8,128)(2,1)S(1)} %bitcast.87, f32[8,768,3,192]{1,3,2,0:T(8,128)} %copy-done.2, f32[8,3,192]{2,1,0:T(4,128)S(1)} %select_maximum_fusion.2, pred[192,768]{1,0:T(8,128)(4,1)S(1)} %compare_and_fusion.2, ...), kind=kOutput, calls=%fused_computation.9.clone.1 | convolution fusion | flops 471564288 | bytes 17485824 | tf_op jit(solution)/shard_map/while/body/eval_jaxpr/kgqc,kcd->kgqd/dot_general | solution.py:58
  278.9 1.7 divide_convert_fusion
  280.6 3.4 fusion.15
  285.4 4.7 %fusion.32 = (bf16[16,55296]{1,0:T(8,128)(2,1)}, bf16[16,55296]{1,0:T(8,128)(2,1)}, bf16[16,55296]{1,0:T(8,128)(2,1)S(1)}) fusion(bf16[16,362496]{1,0:T(8,128)(2,1)} %reshape.228), kind=kLoop, calls=%fused_computation.78 | loop fusion | bytes 10616832 | tf_op jit(solution)/shard_map/slice | solution.py:153
  290.0 4.8 %reshape.226 = bf16[576,1536]{1,0:T(8,128)(2,1)} reshape(bf16[16,55296]{1,0:T(8,128)(2,1)} %get-tuple-element.234) | data formatting | bytes 3538944 | tf_op jit(solution)/shard_map/reshape | solution.py:153
  294.8 4.8 %reshape.227 = bf16[576,1536]{1,0:T(8,128)(2,1)} reshape(bf16[16,55296]{1,0:T(8,128)(2,1)} %get-tuple-element.235) | data formatting | bytes 3538944 | tf_op jit(solution)/shard_map/reshape | solution.py:153
  299.7 3.7 reshape.225
  303.3 16.0 %all-gather.4.cloned.1.call-done = bf16[1536,1536]{1,0:T(8,128)(2,1)} async-done(((bf16[192,1536]{1,0:T(8,128)(2,1)}), bf16[1536,1536]{1,0:T(8,128)(2,1)}) %all-gather.4.cloned.1.call-update) | async-done | bytes 4718608 | tf_op jit(solution)/shard_map/all_gather | solution.py:182
  319.4 7.7 %fusion.43 = f32[1536,576]{0,1:T(8,128)} fusion(bf16[1536,1536]{1,0:T(8,128)(2,1)} %all-gather.4.cloned.1.call-done, bf16[576,1536]{1,0:T(8,128)(2,1)} %reshape.225), kind=kOutput, calls=%fused_computation.89 | convolution fusion | flops 2717908992 | bytes 10027008 | tf_op jit(solution)/shard_map/dot_general | solution.py:67
  327.0 13.3 %convolution_convert_fusion = bf16[1536,1536]{1,0:T(8,128)(2,1)} fusion(bf16[576,1536]{1,0:T(8,128)(2,1)} %reshape.227, f32[1536,576]{0,1:T(8,128)} %fusion.43, bf16[1536,1536]{1,0:T(8,128)(2,1)} %all-gather.4.cloned.1.call-done, bf16[576,1536]{1,0:T(8,128)(2,1)S(1)} %copy-done.5), kind=kOutput, calls=%fused_computation.22 | convolution fusion | flops 5443485696 | bytes 16515072 | tf_op jit(solution)/shard_map/dot_general | solution.py:70
  342.1 37.5 %reduce-scatter.2.cloned.1.call-done = bf16[192,1536]{1,0:T(8,128)(2,1)} async-done(((bf16[1536,1536]{1,0:T(8,128)(2,1)}), bf16[192,1536]{1,0:T(8,128)(2,1)}) %reduce-scatter.2.cloned.1.call-update) | async-done | bytes 589840 | tf_op jit(solution)/shard_map/reduce_scatter | solution.py:184
  379.6 2.0 fusion.22
  (153 shorter events, 29.6 us)
Async XLA Ops:
  7.2 18.3 %copy-start = (bf16[1536,512]{1,0:T(8,128)(2,1)S(1)}, bf16[1536,512]{1,0:T(8,128)(2,1)}, u32[]{:S(2)}) copy-start(bf16[1536,512]{1,0:T(8,128)(2,1)} %param.19) | copy-start | bytes 4718596
  7.2 162.5 %all-gather.6.cloned.1.call-start = ((), (), s32[]{:S(2)}) async-start(), calls=%async_computation.3 | async-start | bytes 12324864 | tf_op jit(solution)/shard_map/all_gather | solution.py:148
  13.3 13.1 %collective-permute-start = (s32[3]{0:T(128)S(1)}, s32[3]{0:T(128)S(1)}, u32[]{:S(2)}, u32[]{:S(2)}) collective-permute-start(s32[3]{0:T(128)S(1)} %pad_add_fusion), channel_id=1, source_target_pairs={{0,1},{1,2},{2,3},{3,4},{4,5},{5,6},{6,7},{7,8},{8,9},{9,10},{10,1... | collective-permute-start | bytes 44 | tf_op jit(solution)/shard_map/ppermute | solution.py:93
  20.0 5.4 %copy-start.12 = (bf16[192,1536]{1,0:T(8,128)(2,1)S(1)}, bf16[192,1536]{1,0:T(8,128)(2,1)}, u32[]{:S(2)}) copy-start(bf16[192,1536]{1,0:T(8,128)(2,1)} %param.15) | copy-start | bytes 1769476
  20.0 5.4 %copy-start.17 = (f32[1536]{0:T(1024)S(1)}, f32[1536]{0:T(1024)}, u32[]{:S(2)}) copy-start(f32[1536]{0:T(1024)} %param.17) | copy-start | bytes 18436
  25.5 55.2 %copy-start.10 = (bf16[192,512]{1,0:T(8,128)(2,1)}, bf16[192,512]{1,0:T(8,128)(2,1)S(1)}, u32[]{:S(2)}) copy-start(bf16[192,512]{1,0:T(8,128)(2,1)S(1)} %convolution_convert_fusion.1) | copy-start | bytes 589828
  25.5 0.8 copy-start.15
  32.3 6.8 %collective-permute-start.1 = (s32[3]{0:T(128)S(1)}, s32[3]{0:T(128)S(1)}, u32[]{:S(2)}, u32[]{:S(2)}) collective-permute-start(s32[3]{0:T(128)S(1)} %broadcast_select_fusion), channel_id=1, source_target_pairs={{0,2},{1,3},{2,4},{3,5},{4,6},{5,7},{6,8},{7,9},{8,10},{9,11},{10,... | collective-permute-start | bytes 44 | tf_op jit(solution)/shard_map/ppermute | solution.py:93
  45.6 5.7 %collective-permute-start.2 = (s32[3]{0:T(128)S(1)}, s32[3]{0:T(128)S(1)}, u32[]{:S(2)}, u32[]{:S(2)}) collective-permute-start(s32[3]{0:T(128)S(1)} %broadcast_select_fusion.1), channel_id=1, source_target_pairs={{0,4},{1,5},{2,6},{3,7},{4,8},{5,9},{6,10},{7,11},{8,12},{9,13},{1... | collective-permute-start | bytes 44 | tf_op jit(solution)/shard_map/ppermute | solution.py:93
  58.6 7.0 %collective-permute-start.3 = (s32[3]{0:T(128)S(1)}, s32[3]{0:T(128)S(1)}, u32[]{:S(2)}, u32[]{:S(2)}) collective-permute-start(s32[3]{0:T(128)S(1)} %broadcast_select_fusion.2), channel_id=1, source_target_pairs={{0,8},{1,9},{2,10},{3,11},{4,12},{5,13},{6,14},{7,15},{16,24},{17,... | collective-permute-start | bytes 44 | tf_op jit(solution)/shard_map/ppermute | solution.py:93
  72.6 5.1 %collective-permute-start.4 = (s32[3]{0:T(128)S(1)}, s32[3]{0:T(128)S(1)}, u32[]{:S(2)}, u32[]{:S(2)}) collective-permute-start(s32[3]{0:T(128)S(1)} %broadcast_select_fusion.3), channel_id=1, source_target_pairs={{0,1},{1,2},{2,3},{3,4},{4,5},{5,6},{6,7},{7,8},{8,9},{9,10},{10,1... | collective-permute-start | bytes 44 | tf_op jit(solution)/shard_map/ppermute | solution.py:99
  81.8 237.6 %all-gather.4.cloned.1.call-start = ((), (), s32[]{:S(2)}) async-start(), calls=%async_computation.1 | async-start | bytes 5308416 | tf_op jit(solution)/shard_map/all_gather | solution.py:182
  81.8 4.6 %copy-start.16 = (f32[64]{0:T(128)S(1)}, f32[64]{0:T(128)}, u32[]{:S(2)}) copy-start(f32[64]{0:T(128)} %param.21) | copy-start | bytes 772
  208.8 5.3 %copy-start.2 = (f32[8,768,3,192]{1,3,2,0:T(8,128)}, f32[8,768,3,192]{1,3,2,0:T(8,128)S(1)}, u32[]{:S(2)}) copy-start(f32[8,768,3,192]{1,3,2,0:T(8,128)S(1)} %get-tuple-element.337) | copy-start | bytes 42467332 | tf_op jit(solution)/shard_map/while
  208.8 5.3 %copy-start.8 = (f32[8,3,192]{2,1,0:T(4,128)S(1)}, f32[8,3,192]{2,1,0:T(4,128)}, u32[]{:S(2)}) copy-start(f32[8,3,192]{2,1,0:T(4,128)} %get-tuple-element.356) | copy-start | bytes 55300 | tf_op jit(solution)/shard_map/while
  208.8 5.3 %copy-start.6 = (f32[8,3,192,64]{2,3,1,0:T(8,128)S(1)}, f32[8,3,192,64]{2,3,1,0:T(8,128)}, u32[]{:S(2)}) copy-start(f32[8,3,192,64]{2,3,1,0:T(8,128)} %get-tuple-element.357) | copy-start | bytes 3538948 | tf_op jit(solution)/shard_map/while
  214.1 7.1 %copy-start.9 = (f32[8,3,192]{2,1,0:T(4,128)}, f32[8,3,192]{2,1,0:T(4,128)S(1)}, u32[]{:S(2)}) copy-start(f32[8,3,192]{2,1,0:T(4,128)S(1)} %get-tuple-element.369) | copy-start | bytes 55300 | tf_op jit(solution)/shard_map/while
  221.2 1.2 copy-start.7
  227.6 5.3 %copy-start.2 = (f32[8,768,3,192]{1,3,2,0:T(8,128)}, f32[8,768,3,192]{1,3,2,0:T(8,128)S(1)}, u32[]{:S(2)}) copy-start(f32[8,768,3,192]{1,3,2,0:T(8,128)S(1)} %get-tuple-element.337) | copy-start | bytes 42467332 | tf_op jit(solution)/shard_map/while
  227.6 5.3 %copy-start.8 = (f32[8,3,192]{2,1,0:T(4,128)S(1)}, f32[8,3,192]{2,1,0:T(4,128)}, u32[]{:S(2)}) copy-start(f32[8,3,192]{2,1,0:T(4,128)} %get-tuple-element.356) | copy-start | bytes 55300 | tf_op jit(solution)/shard_map/while
  227.6 5.3 %copy-start.6 = (f32[8,3,192,64]{2,3,1,0:T(8,128)S(1)}, f32[8,3,192,64]{2,3,1,0:T(8,128)}, u32[]{:S(2)}) copy-start(f32[8,3,192,64]{2,3,1,0:T(8,128)} %get-tuple-element.357) | copy-start | bytes 3538948 | tf_op jit(solution)/shard_map/while
  232.9 7.1 %copy-start.9 = (f32[8,3,192]{2,1,0:T(4,128)}, f32[8,3,192]{2,1,0:T(4,128)S(1)}, u32[]{:S(2)}) copy-start(f32[8,3,192]{2,1,0:T(4,128)S(1)} %get-tuple-element.369) | copy-start | bytes 55300 | tf_op jit(solution)/shard_map/while
  240.1 1.2 copy-start.7
  246.4 5.3 %copy-start.2 = (f32[8,768,3,192]{1,3,2,0:T(8,128)}, f32[8,768,3,192]{1,3,2,0:T(8,128)S(1)}, u32[]{:S(2)}) copy-start(f32[8,768,3,192]{1,3,2,0:T(8,128)S(1)} %get-tuple-element.337) | copy-start | bytes 42467332 | tf_op jit(solution)/shard_map/while
  246.5 5.3 %copy-start.8 = (f32[8,3,192]{2,1,0:T(4,128)S(1)}, f32[8,3,192]{2,1,0:T(4,128)}, u32[]{:S(2)}) copy-start(f32[8,3,192]{2,1,0:T(4,128)} %get-tuple-element.356) | copy-start | bytes 55300 | tf_op jit(solution)/shard_map/while
  246.5 5.3 %copy-start.6 = (f32[8,3,192,64]{2,3,1,0:T(8,128)S(1)}, f32[8,3,192,64]{2,3,1,0:T(8,128)}, u32[]{:S(2)}) copy-start(f32[8,3,192,64]{2,3,1,0:T(8,128)} %get-tuple-element.357) | copy-start | bytes 3538948 | tf_op jit(solution)/shard_map/while
  251.8 7.1 %copy-start.9 = (f32[8,3,192]{2,1,0:T(4,128)}, f32[8,3,192]{2,1,0:T(4,128)S(1)}, u32[]{:S(2)}) copy-start(f32[8,3,192]{2,1,0:T(4,128)S(1)} %get-tuple-element.369) | copy-start | bytes 55300 | tf_op jit(solution)/shard_map/while
  258.9 1.2 copy-start.7
  265.3 5.3 %copy-start.2 = (f32[8,768,3,192]{1,3,2,0:T(8,128)}, f32[8,768,3,192]{1,3,2,0:T(8,128)S(1)}, u32[]{:S(2)}) copy-start(f32[8,768,3,192]{1,3,2,0:T(8,128)S(1)} %get-tuple-element.337) | copy-start | bytes 42467332 | tf_op jit(solution)/shard_map/while
  265.3 5.3 %copy-start.8 = (f32[8,3,192]{2,1,0:T(4,128)S(1)}, f32[8,3,192]{2,1,0:T(4,128)}, u32[]{:S(2)}) copy-start(f32[8,3,192]{2,1,0:T(4,128)} %get-tuple-element.356) | copy-start | bytes 55300 | tf_op jit(solution)/shard_map/while
  265.3 5.3 %copy-start.6 = (f32[8,3,192,64]{2,3,1,0:T(8,128)S(1)}, f32[8,3,192,64]{2,3,1,0:T(8,128)}, u32[]{:S(2)}) copy-start(f32[8,3,192,64]{2,3,1,0:T(8,128)} %get-tuple-element.357) | copy-start | bytes 3538948 | tf_op jit(solution)/shard_map/while
  270.6 7.1 %copy-start.9 = (f32[8,3,192]{2,1,0:T(4,128)}, f32[8,3,192]{2,1,0:T(4,128)S(1)}, u32[]{:S(2)}) copy-start(f32[8,3,192]{2,1,0:T(4,128)S(1)} %get-tuple-element.369) | copy-start | bytes 55300 | tf_op jit(solution)/shard_map/while
  277.7 1.2 copy-start.7
  278.9 1.7 copy-start.13
  280.5 3.7 copy-start.14
  284.0 6.0 %copy-start.3 = (bf16[192,1536]{1,0:T(8,128)(2,1)}, bf16[192,1536]{1,0:T(8,128)(2,1)S(1)}, u32[]{:S(2)}) copy-start(bf16[192,1536]{1,0:T(8,128)(2,1)S(1)} %fusion.15) | copy-start | bytes 1769476
  285.3 94.3 %reduce-scatter.2.cloned.1.call-start = ((), (), s32[]{:S(2)}) async-start(), calls=%async_computation.2 | async-start | bytes 5308416 | tf_op jit(solution)/shard_map/reduce_scatter | solution.py:184
  303.3 23.7 %copy-start.5 = (bf16[576,1536]{1,0:T(8,128)(2,1)S(1)}, bf16[576,1536]{1,0:T(8,128)(2,1)}, u32[]{:S(2)}) copy-start(bf16[576,1536]{1,0:T(8,128)(2,1)} %reshape.226) | copy-start | bytes 5308420
  340.4 0.9 copy-start.11
  340.4 39.2 %copy-start.4 = (bf16[192,1536]{1,0:T(8,128)(2,1)S(1)}, bf16[192,1536]{1,0:T(8,128)(2,1)}, u32[]{:S(2)}) copy-start(bf16[192,1536]{1,0:T(8,128)(2,1)} %copy-done.3) | copy-start | bytes 1769476
  341.3 40.3 %copy-start.1 = (bf16[1536,512]{1,0:T(8,128)(2,1)S(1)}, bf16[1536,512]{1,0:T(8,128)(2,1)}, u32[]{:S(2)}) copy-start(bf16[1536,512]{1,0:T(8,128)(2,1)} %param.19) | copy-start | bytes 4718596
Sparse Core Ops, SparseCore 0:
  81.9 87.7 all-gather.5
  285.4 33.8 all-gather.3
  340.5 38.9 reduce-scatter.1
where the time goes:
time: 389 us; the launch traced here: 388 us
  waiting for transfers between devices  139 us (36%)
  local copies, waits for them, and re-layouts  78 us (20%)
  matrix products  71.9 us (18%)
  other arithmetic  42.9 us (11%)
  between operations  32.2 us (8%)
  starting transfers between devices  23.4 us (6%)
    all_gather x1, waiting for transfers between devices, per_device(): lax.all_gather(jnp.concatenate([p.reshape(-1) for p in pieces]), 'hid', a...  82.5 us
    reduce_scatter x1, waiting for transfers between devices, per_device(): lax.psum_scatter(unit_sum.astype(jnp.bfloat16), 'req', scatter_dimension=...  37.5 us
    dot_general x4, matrix products, key_block(): jnp.einsum('kgqc,kcd->kgqd', weights.astype(jnp.bfloat16), v_grid, prefer...  28.4 us
    reshape x4, local copies, waits for them, and re-layouts, per_device(): bundle[:, cuts[i]:cuts[i + 1]]  19.7 us
    ppermute x4, starting transfers between devices, group_positions(): got = lax.ppermute(summary, axis, pairs)  19.5 us
    reduce_sum x4, other arithmetic, key_block(): new_total = run_total * factor + jnp.sum(weights, axis=-1)  18.8 us
    all_gather x1, waiting for transfers between devices, per_device(): gathered = lax.all_gather(mlp_in, 'req', axis=0, tiled=True)  16 us
    all_gather x1, local copies, waits for them, and re-layouts, per_device(): lax.all_gather(jnp.concatenate([p.reshape(-1) for p in pieces]), 'hid', a...  15.1 us
  transfers between devices with their start and end apart: 8, of which 7 were waited for; matrix products, arithmetic and copies ran while one was open for 9% of the time, Pallas kernels for 0%

commit v1 on v0

--- a/solution.py
+++ b/solution.py
@@ -179,7 +179,12 @@
     )
     after_f32 = lax.optimization_barrier(after_attn).astype(jnp.float32)
     mlp_in = rms_scale(after_f32, ffn_gain).astype(jnp.bfloat16)
-    gathered = lax.all_gather(mlp_in, "req", axis=0, tiled=True)
+    ring = [mlp_in]
+    for hop in range(7):
+        ring.append(lax.ppermute(ring[-1], "req", [(dev, (dev + 1) % 8) for dev in range(8)]))
+    gathered = jnp.roll(
+        jnp.concatenate(ring[::-1], axis=0), (lax.axis_index("req") + 1) * ring[0].shape[0], axis=0
+    )
     unit_sum = unit_terms((gate_rows, up_rows, down_rows), gathered)
     own_share = lax.psum_scatter(
         unit_sum.astype(jnp.bfloat16), "req", scatter_dimension=0, tiled=True

time: 389 us -> 446 us (1.15)
  waiting for transfers between devices: 139 us -> 186 us
  local copies, waits for them, and re-layouts: 78 us -> 90.1 us
    ppermute x0 -> x7, waiting for transfers between devices: none -> 63.5 us  [per_device(): lax.ppermute(ring[-1], 'req', [(dev, (dev + 1) % 8) for dev in range(8)])]
    all_gather x1 -> x0, waiting for transfers between devices: 16 us -> none  [per_device(): gathered = lax.all_gather(mlp_in, 'req', axis=0, tiled=True)]
    unnamed x27 -> x41, local copies, waits for them, and re-layouts: 1.04 us -> 11.9 us
  transfers between devices with their start and end apart: 8 -> 14, of which waited for: 7 -> 12; matrix products, arithmetic and copies ran while one was open for 9% -> 8% of each run, Pallas kernels for 0% -> 0%
where the time goes in v1:
time: 446 us; the launch traced here: 445 us
  waiting for transfers between devices  186 us (42%)
  local copies, waits for them, and re-layouts  90.1 us (20%)
  matrix products  69.7 us (16%)
  other arithmetic  42.4 us (10%)
  between operations  32.5 us (7%)
  starting transfers between devices  23.4 us (5%)
    all_gather x1, waiting for transfers between devices, per_device(): lax.all_gather(jnp.concatenate([p.reshape(-1) for p in pieces]), 'hid', a...  82.5 us
    ppermute x7, waiting for transfers between devices, per_device(): lax.ppermute(ring[-1], 'req', [(dev, (dev + 1) % 8) for dev in range(8)])  63.5 us
    reduce_scatter x1, waiting for transfers between devices, per_device(): lax.psum_scatter(unit_sum.astype(jnp.bfloat16), 'req', scatter_dimension=...  37 us
    dot_general x4, matrix products, key_block(): jnp.einsum('kgqc,kcd->kgqd', weights.astype(jnp.bfloat16), v_grid, prefer...  28.4 us
    reshape x4, local copies, waits for them, and re-layouts, per_device(): bundle[:, cuts[i]:cuts[i + 1]]  20.8 us
    ppermute x4, starting transfers between devices, group_positions(): got = lax.ppermute(summary, axis, pairs)  19.5 us
    reduce_sum x4, other arithmetic, key_block(): new_total = run_total * factor + jnp.sum(weights, axis=-1)  18.8 us
    all_gather x1, local copies, waits for them, and re-layouts, per_device(): lax.all_gather(jnp.concatenate([p.reshape(-1) for p in pieces]), 'hid', a...  15.1 us
  transfers between devices with their start and end apart: 14, of which 12 were waited for; matrix products, arithmetic and copies ran while one was open for 8% of the time, Pallas kernels for 0%

profile of v1, /device:TPU:0, one launch (start us, length us, event | category | flops | bytes accessed | tf_op | source)
XLA Modules:
  0.0 444.7 jit_solution(11956148769234451914)
XLA Ops:
  8.7 2.0 fusion.33
  13.3 3.9 collective-permute-start
  23.3 2.1 convolution_convert_fusion.1
  32.2 5.5 %collective-permute-start.1 = (s32[3]{0:T(128)S(1)}, s32[3]{0:T(128)S(1)}, u32[]{:S(2)}, u32[]{:S(2)}) collective-permute-start(s32[3]{0:T(128)S(1)} %broadcast_select_fusion), channel_id=1, source_target_pairs={{0,2},{1,3},{2,4},{3,5},{4,6},{5,7},{6,8},{7,9},{8,10},{9,11},{10,... | collective-permute-start | bytes 44 | tf_op jit(solution)/shard_map/ppermute | solution.py:93
  42.9 1.9 broadcast_select_fusion.1
  45.4 4.4 %collective-permute-start.2 = (s32[3]{0:T(128)S(1)}, s32[3]{0:T(128)S(1)}, u32[]{:S(2)}, u32[]{:S(2)}) collective-permute-start(s32[3]{0:T(128)S(1)} %broadcast_select_fusion.1), channel_id=1, source_target_pairs={{0,4},{1,5},{2,6},{3,7},{4,8},{5,9},{6,10},{7,11},{8,12},{9,13},{1... | collective-permute-start | bytes 44 | tf_op jit(solution)/shard_map/ppermute | solution.py:93
  55.2 2.6 broadcast_select_fusion.2
  58.4 5.7 %collective-permute-start.3 = (s32[3]{0:T(128)S(1)}, s32[3]{0:T(128)S(1)}, u32[]{:S(2)}, u32[]{:S(2)}) collective-permute-start(s32[3]{0:T(128)S(1)} %broadcast_select_fusion.2), channel_id=1, source_target_pairs={{0,8},{1,9},{2,10},{3,11},{4,12},{5,13},{6,14},{7,15},{16,24},{17,... | collective-permute-start | bytes 44 | tf_op jit(solution)/shard_map/ppermute | solution.py:93
  69.2 3.3 broadcast_select_fusion.3
  72.5 3.8 collective-permute-start.4
  81.8 4.3 fusion.39
  87.1 82.5 %all-gather.3.cloned.1.call-done = bf16[5799936]{0:T(1024)(128)(2,1)} async-done(((bf16[362496]{0:T(1024)(128)(2,1)}), bf16[5799936]{0:T(1024)(128)(2,1)}) %all-gather.3.cloned.1.call-update) | async-done | bytes 11599888 | tf_op jit(solution)/shard_map/all_gather | solution.py:148
  169.6 15.1 %reshape.228 = bf16[16,362496]{1,0:T(8,128)(2,1)} reshape(bf16[5799936]{0:T(1024)(128)(2,1)} %all-gather.3.cloned.1.call-done) | data formatting | bytes 23199744 | tf_op jit(solution)/shard_map/all_gather | solution.py:148
  184.6 6.4 %slice.164 = bf16[16,196608]{1,0:T(8,128)(2,1)} slice(bf16[16,362496]{1,0:T(8,128)(2,1)} %reshape.228), slice={[0:16], [0:196608]} | slice | bytes 12582912 | tf_op jit(solution)/shard_map/slice | solution.py:153
  191.1 6.4 %reshape.223 = bf16[3072,1024]{1,0:T(8,128)(2,1)} reshape(bf16[16,196608]{1,0:T(8,128)(2,1)} %slice.164) | data formatting | bytes 12582912 | tf_op jit(solution)/shard_map/reshape | solution.py:153
  197.5 6.0 %fusion.45 = (bf16[3072,512]{1,0:T(8,128)(2,1)}, bf16[3072,512]{1,0:T(8,128)(2,1)}) fusion(bf16[3072,1024]{1,0:T(8,128)(2,1)} %reshape.223), kind=kLoop, calls=%fused_computation.102 | loop fusion | bytes 12582912 | tf_op jit(solution)/shard_map/slice | solution.py:158
  203.4 75.2 %while.18 = (s32[]{:T(128)}, f32[8,3,192]{2,1,0:T(4,128)S(1)}, f32[8,3,192]{2,1,0:T(4,128)S(1)}, f32[8,3,192,64]{2,3,1,0:T(8,128)}, s32[192]{0:T(256)S(1)}, /*in...) while((s32[]{:T(128)}, f32[8,3,192]{2,1,0:T(4,128)S(1)}, ...), condition=%wide.region_9.10_spmd.clone, body=%wide.region_6.9_spmd.clone.sunk | while | flops 953327040 | bytes 120234520 | solution.py:170
  203.6 1.5 constant_dynamic-slice_fusion.3
  205.7 3.0 fusion.79
  208.7 4.7 %fusion.80 = f32[8,3,192]{2,1,0:T(4,128)S(1)} fusion(f32[8,768,3,192]{1,3,2,0:T(8,128)S(1)} %get-tuple-element.337, f32[8,3,192]{2,1,0:T(4,128)S(1)} %select_maximum_fusion.2, pred[192,768]{1,0:T(8,128)(4,1)S(1)} %compare_and_fusion.2), kind=kLoop, calls=%fused_computation.5.clone.1 | loop fusion | flops 17690112 | bytes 14340096 | tf_op jit(solution)/shard_map/while/body/eval_jaxpr/reduce_sum | solution.py:57
  214.0 7.1 %fusion.82 = f32[8,3,192,64]{2,3,1,0:T(8,128)S(1)} fusion(f32[8,3,192,64]{2,3,1,0:T(8,128)S(1)} %copy-done.6, bf16[8,768,64,1]{1,2,3,0:T(8,128)(2,1)S(1)} %bitcast.85, f32[8,768,3,192]{1,3,2,0:T(8,128)} %copy-done.2, f32[8,3,192]{2,1,0:T(4,128)S(1)} %select_maximum_fusion.2, pred[192,768]{1,0:T(8,128)(4,1)S(1)} %compare_and_fusion.2, ...), kind=kOutput, calls=%fused_computation.9.clone.1 | convolution fusion | flops 471564288 | bytes 17485824 | tf_op jit(solution)/shard_map/while/body/eval_jaxpr/kgqc,kcd->kgqd/dot_general | solution.py:58
  222.4 1.5 constant_dynamic-slice_fusion.3
  224.5 3.0 fusion.79
  227.5 4.7 %fusion.80 = f32[8,3,192]{2,1,0:T(4,128)S(1)} fusion(f32[8,768,3,192]{1,3,2,0:T(8,128)S(1)} %get-tuple-element.337, f32[8,3,192]{2,1,0:T(4,128)S(1)} %select_maximum_fusion.2, pred[192,768]{1,0:T(8,128)(4,1)S(1)} %compare_and_fusion.2), kind=kLoop, calls=%fused_computation.5.clone.1 | loop fusion | flops 17690112 | bytes 14340096 | tf_op jit(solution)/shard_map/while/body/eval_jaxpr/reduce_sum | solution.py:57
  232.8 7.1 %fusion.82 = f32[8,3,192,64]{2,3,1,0:T(8,128)S(1)} fusion(f32[8,3,192,64]{2,3,1,0:T(8,128)S(1)} %copy-done.6, bf16[8,768,64,1]{1,2,3,0:T(8,128)(2,1)S(1)} %bitcast.85, f32[8,768,3,192]{1,3,2,0:T(8,128)} %copy-done.2, f32[8,3,192]{2,1,0:T(4,128)S(1)} %select_maximum_fusion.2, pred[192,768]{1,0:T(8,128)(4,1)S(1)} %compare_and_fusion.2, ...), kind=kOutput, calls=%fused_computation.9.clone.1 | convolution fusion | flops 471564288 | bytes 17485824 | tf_op jit(solution)/shard_map/while/body/eval_jaxpr/kgqc,kcd->kgqd/dot_general | solution.py:58
  243.3 3.0 fusion.79
  246.3 4.7 %fusion.80 = f32[8,3,192]{2,1,0:T(4,128)S(1)} fusion(f32[8,768,3,192]{1,3,2,0:T(8,128)S(1)} %get-tuple-element.337, f32[8,3,192]{2,1,0:T(4,128)S(1)} %select_maximum_fusion.2, pred[192,768]{1,0:T(8,128)(4,1)S(1)} %compare_and_fusion.2), kind=kLoop, calls=%fused_computation.5.clone.1 | loop fusion | flops 17690112 | bytes 14340096 | tf_op jit(solution)/shard_map/while/body/eval_jaxpr/reduce_sum | solution.py:57
  251.5 7.1 %fusion.82 = f32[8,3,192,64]{2,3,1,0:T(8,128)S(1)} fusion(f32[8,3,192,64]{2,3,1,0:T(8,128)S(1)} %copy-done.6, bf16[8,768,64,1]{1,2,3,0:T(8,128)(2,1)S(1)} %bitcast.85, f32[8,768,3,192]{1,3,2,0:T(8,128)} %copy-done.2, f32[8,3,192]{2,1,0:T(4,128)S(1)} %select_maximum_fusion.2, pred[192,768]{1,0:T(8,128)(4,1)S(1)} %compare_and_fusion.2, ...), kind=kOutput, calls=%fused_computation.9.clone.1 | convolution fusion | flops 471564288 | bytes 17485824 | tf_op jit(solution)/shard_map/while/body/eval_jaxpr/kgqc,kcd->kgqd/dot_general | solution.py:58
  262.0 3.0 fusion.79
  265.1 4.7 %fusion.80 = f32[8,3,192]{2,1,0:T(4,128)S(1)} fusion(f32[8,768,3,192]{1,3,2,0:T(8,128)S(1)} %get-tuple-element.337, f32[8,3,192]{2,1,0:T(4,128)S(1)} %select_maximum_fusion.2, pred[192,768]{1,0:T(8,128)(4,1)S(1)} %compare_and_fusion.2), kind=kLoop, calls=%fused_computation.5.clone.1 | loop fusion | flops 17690112 | bytes 14340096 | tf_op jit(solution)/shard_map/while/body/eval_jaxpr/reduce_sum | solution.py:57
  270.3 7.1 %fusion.82 = f32[8,3,192,64]{2,3,1,0:T(8,128)S(1)} fusion(f32[8,3,192,64]{2,3,1,0:T(8,128)S(1)} %copy-done.6, bf16[8,768,64,1]{1,2,3,0:T(8,128)(2,1)S(1)} %bitcast.85, f32[8,768,3,192]{1,3,2,0:T(8,128)} %copy-done.2, f32[8,3,192]{2,1,0:T(4,128)S(1)} %select_maximum_fusion.2, pred[192,768]{1,0:T(8,128)(4,1)S(1)} %compare_and_fusion.2, ...), kind=kOutput, calls=%fused_computation.9.clone.1 | convolution fusion | flops 471564288 | bytes 17485824 | tf_op jit(solution)/shard_map/while/body/eval_jaxpr/kgqc,kcd->kgqd/dot_general | solution.py:58
  278.6 1.6 divide_convert_fusion
  280.2 3.6 fusion.19
  284.3 10.5 %collective-permute-done.5 = bf16[192,1536]{1,0:T(8,128)(2,1)S(1)} collective-permute-done((bf16[192,1536]{1,0:T(8,128)(2,1)S(1)}, bf16[192,1536]{1,0:T(8,128)(2,1)S(1)}, u32[]{:S(2)}, u32[]{:S(2)}) %collective-permute-start.5) | collective-permute-done | bytes 589856 | tf_op jit(solution)/shard_map/ppermute | solution.py:184
  294.8 10.5 %collective-permute-done.6 = bf16[192,1536]{1,0:T(8,128)(2,1)S(1)} collective-permute-done((bf16[192,1536]{1,0:T(8,128)(2,1)S(1)}, bf16[192,1536]{1,0:T(8,128)(2,1)S(1)}, u32[]{:S(2)}, u32[]{:S(2)}) %collective-permute-start.6) | collective-permute-done | bytes 589856 | tf_op jit(solution)/shard_map/ppermute | solution.py:184
  305.3 10.5 %collective-permute-done.7 = bf16[192,1536]{1,0:T(8,128)(2,1)S(1)} collective-permute-done((bf16[192,1536]{1,0:T(8,128)(2,1)S(1)}, bf16[192,1536]{1,0:T(8,128)(2,1)S(1)}, u32[]{:S(2)}, u32[]{:S(2)}) %collective-permute-start.7) | collective-permute-done | bytes 589856 | tf_op jit(solution)/shard_map/ppermute | solution.py:184
  315.8 10.5 %collective-permute-done.8 = bf16[192,1536]{1,0:T(8,128)(2,1)S(1)} collective-permute-done((bf16[192,1536]{1,0:T(8,128)(2,1)S(1)}, bf16[192,1536]{1,0:T(8,128)(2,1)S(1)}, u32[]{:S(2)}, u32[]{:S(2)}) %collective-permute-start.8) | collective-permute-done | bytes 589856 | tf_op jit(solution)/shard_map/ppermute | solution.py:184
  326.3 10.6 %collective-permute-done.9 = bf16[192,1536]{1,0:T(8,128)(2,1)} collective-permute-done((bf16[192,1536]{1,0:T(8,128)(2,1)S(1)}, bf16[192,1536]{1,0:T(8,128)(2,1)}, u32[]{:S(2)}, u32[]{:S(2)}) %collective-permute-start.9) | collective-permute-done | bytes 589856 | tf_op jit(solution)/shard_map/ppermute | solution.py:184
  337.0 10.8 %collective-permute-done.10 = bf16[192,1536]{1,0:T(8,128)(2,1)} collective-permute-done((bf16[192,1536]{1,0:T(8,128)(2,1)}, bf16[192,1536]{1,0:T(8,128)(2,1)}, u32[]{:S(2)}, u32[]{:S(2)}) %collective-permute-start.10) | collective-permute-done | bytes 589856 | tf_op jit(solution)/shard_map/ppermute | solution.py:184
  347.8 5.0 %fusion.44 = (bf16[16,55296]{1,0:T(8,128)(2,1)}, bf16[16,55296]{1,0:T(8,128)(2,1)}, bf16[16,55296]{1,0:T(8,128)(2,1)}) fusion(bf16[16,362496]{1,0:T(8,128)(2,1)} %reshape.228), kind=kLoop, calls=%fused_computation.101 | loop fusion | bytes 10616832 | tf_op jit(solution)/shard_map/slice | solution.py:153
  352.7 4.8 %reshape.225 = bf16[576,1536]{1,0:T(8,128)(2,1)} reshape(bf16[16,55296]{1,0:T(8,128)(2,1)} %get-tuple-element.234) | data formatting | bytes 3538944 | tf_op jit(solution)/shard_map/reshape | solution.py:153
  357.5 4.8 %reshape.227 = bf16[576,1536]{1,0:T(8,128)(2,1)} reshape(bf16[16,55296]{1,0:T(8,128)(2,1)} %get-tuple-element.235) | data formatting | bytes 3538944 | tf_op jit(solution)/shard_map/reshape | solution.py:153
  362.3 4.8 %reshape.226 = bf16[576,1536]{1,0:T(8,128)(2,1)} reshape(bf16[16,55296]{1,0:T(8,128)(2,1)} %get-tuple-element.236) | data formatting | bytes 3538944 | tf_op jit(solution)/shard_map/reshape | solution.py:153
  374.7 3.7 copy-done.12
  378.4 4.7 %fusion.15 = f32[1536,576]{0,1:T(8,128)} fusion(bf16[576,1536]{1,0:T(8,128)(2,1)S(1)} %copy-done.3, bf16[3072,1536]{1,0:T(8,128)(2,1)S(1)} %constant_dynamic-update-slice_fusion, s32[]{:T(128)S(6)} %select_n.125), kind=kOutput, calls=%fused_computation.23 | convolution fusion | flops 2717908992 | bytes 10027012 | tf_op jit(solution)/shard_map/dot_general | solution.py:68
  383.1 13.9 %convolution_convert_fusion = bf16[1536,1536]{1,0:T(8,128)(2,1)} fusion(bf16[576,1536]{1,0:T(8,128)(2,1)} %reshape.227, f32[1536,576]{0,1:T(8,128)} %fusion.15, bf16[576,1536]{1,0:T(8,128)(2,1)} %reshape.225, bf16[3072,1536]{1,0:T(8,128)(2,1)} %copy-done.12, s32[]{:T(128)S(6)} %select_n.125), kind=kOutput, calls=%fused_computation.22 | convolution fusion | flops 5443485696 | bytes 16515076 | tf_op jit(solution)/shard_map/dot_general | solution.py:70
  398.8 37.0 %reduce-scatter.2.cloned.1.call-done = bf16[192,1536]{1,0:T(8,128)(2,1)} async-done(((bf16[1536,1536]{1,0:T(8,128)(2,1)}), bf16[192,1536]{1,0:T(8,128)(2,1)}) %reduce-scatter.2.cloned.1.call-update) | async-done | bytes 589840 | tf_op jit(solution)/shard_map/reduce_scatter | solution.py:189
  435.8 2.0 fusion.31
  (164 shorter events, 44.6 us)
Async XLA Ops:
  7.2 18.2 %copy-start = (bf16[1536,512]{1,0:T(8,128)(2,1)S(1)}, bf16[1536,512]{1,0:T(8,128)(2,1)}, u32[]{:S(2)}) copy-start(bf16[1536,512]{1,0:T(8,128)(2,1)} %param.19) | copy-start | bytes 4718596
  7.2 18.2 %copy-start.10 = (bf16[192,1536]{1,0:T(8,128)(2,1)S(1)}, bf16[192,1536]{1,0:T(8,128)(2,1)}, u32[]{:S(2)}) copy-start(bf16[192,1536]{1,0:T(8,128)(2,1)} %param.15) | copy-start | bytes 1769476
  7.2 18.2 %copy-start.15 = (f32[1536]{0:T(1024)S(1)}, f32[1536]{0:T(1024)}, u32[]{:S(2)}) copy-start(f32[1536]{0:T(1024)} %param.17) | copy-start | bytes 18436
  7.2 162.4 %all-gather.3.cloned.1.call-start = ((), (), s32[]{:S(2)}) async-start(), calls=%async_computation.2 | async-start | bytes 12324864 | tf_op jit(solution)/shard_map/all_gather | solution.py:148
  13.3 13.1 %collective-permute-start = (s32[3]{0:T(128)S(1)}, s32[3]{0:T(128)S(1)}, u32[]{:S(2)}, u32[]{:S(2)}) collective-permute-start(s32[3]{0:T(128)S(1)} %pad_add_fusion), channel_id=1, source_target_pairs={{0,1},{1,2},{2,3},{3,4},{4,5},{5,6},{6,7},{7,8},{8,9},{9,10},{10,1... | collective-permute-start | bytes 44 | tf_op jit(solution)/shard_map/ppermute | solution.py:93
  18.8 7.5 %copy-start.13 = (f32[64]{0:T(128)S(1)}, f32[64]{0:T(128)}, u32[]{:S(2)}) copy-start(f32[64]{0:T(128)} %param.22) | copy-start | bytes 772
  25.4 55.2 %copy-start.8 = (bf16[192,512]{1,0:T(8,128)(2,1)}, bf16[192,512]{1,0:T(8,128)(2,1)S(1)}, u32[]{:S(2)}) copy-start(bf16[192,512]{1,0:T(8,128)(2,1)S(1)} %convolution_convert_fusion.1) | copy-start | bytes 589828
  32.2 6.8 %collective-permute-start.1 = (s32[3]{0:T(128)S(1)}, s32[3]{0:T(128)S(1)}, u32[]{:S(2)}, u32[]{:S(2)}) collective-permute-start(s32[3]{0:T(128)S(1)} %broadcast_select_fusion), channel_id=1, source_target_pairs={{0,2},{1,3},{2,4},{3,5},{4,6},{5,7},{6,8},{7,9},{8,10},{9,11},{10,... | collective-permute-start | bytes 44 | tf_op jit(solution)/shard_map/ppermute | solution.py:93
  45.4 5.7 %collective-permute-start.2 = (s32[3]{0:T(128)S(1)}, s32[3]{0:T(128)S(1)}, u32[]{:S(2)}, u32[]{:S(2)}) collective-permute-start(s32[3]{0:T(128)S(1)} %broadcast_select_fusion.1), channel_id=1, source_target_pairs={{0,4},{1,5},{2,6},{3,7},{4,8},{5,9},{6,10},{7,11},{8,12},{9,13},{1... | collective-permute-start | bytes 44 | tf_op jit(solution)/shard_map/ppermute | solution.py:93
  58.4 7.0 %collective-permute-start.3 = (s32[3]{0:T(128)S(1)}, s32[3]{0:T(128)S(1)}, u32[]{:S(2)}, u32[]{:S(2)}) collective-permute-start(s32[3]{0:T(128)S(1)} %broadcast_select_fusion.2), channel_id=1, source_target_pairs={{0,8},{1,9},{2,10},{3,11},{4,12},{5,13},{6,14},{7,15},{16,24},{17,... | collective-permute-start | bytes 44 | tf_op jit(solution)/shard_map/ppermute | solution.py:93
  72.5 5.1 %collective-permute-start.4 = (s32[3]{0:T(128)S(1)}, s32[3]{0:T(128)S(1)}, u32[]{:S(2)}, u32[]{:S(2)}) collective-permute-start(s32[3]{0:T(128)S(1)} %broadcast_select_fusion.3), channel_id=1, source_target_pairs={{0,1},{1,2},{2,3},{3,4},{4,5},{5,6},{6,7},{7,8},{8,9},{9,10},{10,1... | collective-permute-start | bytes 44 | tf_op jit(solution)/shard_map/ppermute | solution.py:99
  80.6 5.5 %copy-start.4 = (bf16[192,512]{1,0:T(8,128)(2,1)}, bf16[192,512]{1,0:T(8,128)(2,1)S(1)}, u32[]{:S(2)}) copy-start(bf16[192,512]{1,0:T(8,128)(2,1)S(1)} %copy.23) | copy-start | bytes 589828
  81.7 354.2 %reduce-scatter.2.cloned.1.call-start = ((), (), s32[]{:S(2)}) async-start(), calls=%async_computation.1 | async-start | bytes 5308416 | tf_op jit(solution)/shard_map/reduce_scatter | solution.py:189
  81.7 4.6 %copy-start.14 = (f32[64]{0:T(128)S(1)}, f32[64]{0:T(128)}, u32[]{:S(2)}) copy-start(f32[64]{0:T(128)} %param.21) | copy-start | bytes 772
  208.6 5.3 %copy-start.2 = (f32[8,768,3,192]{1,3,2,0:T(8,128)}, f32[8,768,3,192]{1,3,2,0:T(8,128)S(1)}, u32[]{:S(2)}) copy-start(f32[8,768,3,192]{1,3,2,0:T(8,128)S(1)} %get-tuple-element.337) | copy-start | bytes 42467332 | tf_op jit(solution)/shard_map/while
  208.7 5.3 %copy-start.6 = (f32[8,3,192,64]{2,3,1,0:T(8,128)S(1)}, f32[8,3,192,64]{2,3,1,0:T(8,128)}, u32[]{:S(2)}) copy-start(f32[8,3,192,64]{2,3,1,0:T(8,128)} %get-tuple-element.357) | copy-start | bytes 3538948 | tf_op jit(solution)/shard_map/while
  221.1 1.2 copy-start.7
  227.4 5.3 %copy-start.2 = (f32[8,768,3,192]{1,3,2,0:T(8,128)}, f32[8,768,3,192]{1,3,2,0:T(8,128)S(1)}, u32[]{:S(2)}) copy-start(f32[8,768,3,192]{1,3,2,0:T(8,128)S(1)} %get-tuple-element.337) | copy-start | bytes 42467332 | tf_op jit(solution)/shard_map/while
  227.5 5.3 %copy-start.6 = (f32[8,3,192,64]{2,3,1,0:T(8,128)S(1)}, f32[8,3,192,64]{2,3,1,0:T(8,128)}, u32[]{:S(2)}) copy-start(f32[8,3,192,64]{2,3,1,0:T(8,128)} %get-tuple-element.357) | copy-start | bytes 3538948 | tf_op jit(solution)/shard_map/while
  239.9 1.2 copy-start.7
  246.2 5.3 %copy-start.2 = (f32[8,768,3,192]{1,3,2,0:T(8,128)}, f32[8,768,3,192]{1,3,2,0:T(8,128)S(1)}, u32[]{:S(2)}) copy-start(f32[8,768,3,192]{1,3,2,0:T(8,128)S(1)} %get-tuple-element.337) | copy-start | bytes 42467332 | tf_op jit(solution)/shard_map/while
  246.3 5.3 %copy-start.6 = (f32[8,3,192,64]{2,3,1,0:T(8,128)S(1)}, f32[8,3,192,64]{2,3,1,0:T(8,128)}, u32[]{:S(2)}) copy-start(f32[8,3,192,64]{2,3,1,0:T(8,128)} %get-tuple-element.357) | copy-start | bytes 3538948 | tf_op jit(solution)/shard_map/while
  258.6 1.2 copy-start.7
  265.0 5.3 %copy-start.2 = (f32[8,768,3,192]{1,3,2,0:T(8,128)}, f32[8,768,3,192]{1,3,2,0:T(8,128)S(1)}, u32[]{:S(2)}) copy-start(f32[8,768,3,192]{1,3,2,0:T(8,128)S(1)} %get-tuple-element.337) | copy-start | bytes 42467332 | tf_op jit(solution)/shard_map/while
  265.0 5.3 %copy-start.6 = (f32[8,3,192,64]{2,3,1,0:T(8,128)S(1)}, f32[8,3,192,64]{2,3,1,0:T(8,128)}, u32[]{:S(2)}) copy-start(f32[8,3,192,64]{2,3,1,0:T(8,128)} %get-tuple-element.357) | copy-start | bytes 3538948 | tf_op jit(solution)/shard_map/while
  277.4 1.2 copy-start.7
  280.2 3.8 copy-start.11
  284.2 10.5 %collective-permute-start.5 = (bf16[192,1536]{1,0:T(8,128)(2,1)S(1)}, bf16[192,1536]{1,0:T(8,128)(2,1)S(1)}, u32[]{:S(2)}, u32[]{:S(2)}) collective-permute-start(bf16[192,1536]{1,0:T(8,128)(2,1)S(1)} %fusion.30), channel_id=1, source_target_pairs={{0,16},{16,32},{32,48},{48,64},{64,80},{80,96},{96,112},{112,0},{1... | collective-permute-start | bytes 1769480 | tf_op jit(solution)/shard_map/ppermute | solution.py:184
  294.8 10.5 %collective-permute-start.6 = (bf16[192,1536]{1,0:T(8,128)(2,1)S(1)}, bf16[192,1536]{1,0:T(8,128)(2,1)S(1)}, u32[]{:S(2)}, u32[]{:S(2)}) collective-permute-start(bf16[192,1536]{1,0:T(8,128)(2,1)S(1)} %collective-permute-done.5), channel_id=1, source_target_pairs={{0,16},{16,32},{32,48},{48,64},{64,80},{80,96},{96,112},{112,0},{1... | collective-permute-start | bytes 1769480 | tf_op jit(solution)/shard_map/ppermute | solution.py:184
  305.3 10.5 %collective-permute-start.7 = (bf16[192,1536]{1,0:T(8,128)(2,1)S(1)}, bf16[192,1536]{1,0:T(8,128)(2,1)S(1)}, u32[]{:S(2)}, u32[]{:S(2)}) collective-permute-start(bf16[192,1536]{1,0:T(8,128)(2,1)S(1)} %collective-permute-done.6), channel_id=1, source_target_pairs={{0,16},{16,32},{32,48},{48,64},{64,80},{80,96},{96,112},{112,0},{1... | collective-permute-start | bytes 1769480 | tf_op jit(solution)/shard_map/ppermute | solution.py:184
  315.8 10.5 %collective-permute-start.8 = (bf16[192,1536]{1,0:T(8,128)(2,1)S(1)}, bf16[192,1536]{1,0:T(8,128)(2,1)S(1)}, u32[]{:S(2)}, u32[]{:S(2)}) collective-permute-start(bf16[192,1536]{1,0:T(8,128)(2,1)S(1)} %collective-permute-done.7), channel_id=1, source_target_pairs={{0,16},{16,32},{32,48},{48,64},{64,80},{80,96},{96,112},{112,0},{1... | collective-permute-start | bytes 1769480 | tf_op jit(solution)/shard_map/ppermute | solution.py:184
  326.3 10.6 %collective-permute-start.9 = (bf16[192,1536]{1,0:T(8,128)(2,1)S(1)}, bf16[192,1536]{1,0:T(8,128)(2,1)}, u32[]{:S(2)}, u32[]{:S(2)}) collective-permute-start(bf16[192,1536]{1,0:T(8,128)(2,1)S(1)} %collective-permute-done.8), channel_id=1, source_target_pairs={{0,16},{16,32},{32,48},{48,64},{64,80},{80,96},{96,112},{112,0},{1... | collective-permute-start | bytes 1769480 | tf_op jit(solution)/shard_map/ppermute | solution.py:184
  336.9 10.8 %collective-permute-start.10 = (bf16[192,1536]{1,0:T(8,128)(2,1)}, bf16[192,1536]{1,0:T(8,128)(2,1)}, u32[]{:S(2)}, u32[]{:S(2)}) collective-permute-start(bf16[192,1536]{1,0:T(8,128)(2,1)} %collective-permute-done.9), channel_id=1, source_target_pairs={{0,16},{16,32},{32,48},{48,64},{64,80},{80,96},{96,112},{112,0},{1... | collective-permute-start | bytes 1769480 | tf_op jit(solution)/shard_map/ppermute | solution.py:184
  347.8 19.3 %collective-permute-start.11 = (bf16[192,1536]{1,0:T(8,128)(2,1)}, bf16[192,1536]{1,0:T(8,128)(2,1)}, u32[]{:S(2)}, u32[]{:S(2)}) collective-permute-start(bf16[192,1536]{1,0:T(8,128)(2,1)} %collective-permute-done.10), channel_id=1, source_target_pairs={{0,16},{16,32},{32,48},{48,64},{64,80},{80,96},{96,112},{112,0},{1... | collective-permute-start | bytes 1769480 | tf_op jit(solution)/shard_map/ppermute | solution.py:184
  373.0 5.3 %copy-start.3 = (bf16[576,1536]{1,0:T(8,128)(2,1)S(1)}, bf16[576,1536]{1,0:T(8,128)(2,1)}, u32[]{:S(2)}) copy-start(bf16[576,1536]{1,0:T(8,128)(2,1)} %reshape.226) | copy-start | bytes 5308420
  374.7 3.7 copy-start.12
  397.0 0.9 copy-start.5
  397.0 1.0 copy-start.9
  397.0 40.9 %copy-start.1 = (bf16[1536,512]{1,0:T(8,128)(2,1)S(1)}, bf16[1536,512]{1,0:T(8,128)(2,1)}, u32[]{:S(2)}) copy-start(bf16[1536,512]{1,0:T(8,128)(2,1)} %param.19) | copy-start | bytes 4718596
Sparse Core Ops, SparseCore 0:
  81.8 87.7 all-gather.2
  397.2 38.6 reduce-scatter.1
